TPU v7x, 256 devices: a whole 4x4x8 slice. The times are simulated.
256 devices in a mesh: sec: 2 (over x_hi), gy: 16 (over y, x_lo, core), gz: 8 (over z).
Axes of the slice: x: 4 (x_hi: 2, x_lo: 2; x = x_hi * 2 + x_lo), y: 4, z: 8, core: 2. Of those that a mesh axis runs over, the one named last changes fastest.
Arguments:
- populations: float32 [56, 4, 128, 1024], P('sec', None, 'gy', 'gz'), may hold values from 0 to 1, as said below
- solid_mask: int32 [4, 128, 1024], P(None, 'gy', 'gz'), may hold values 0 or 1
- flow_rates: float32 [15], replicated, may hold values from 0.5 to 1.8
- species_rates: float32 [4], replicated, may hold values from 0.5 to 1.8
- cotangents: float32 [56, 4, 128, 1024], P('sec', None, 'gy', 'gz'), may hold values from -6 to 6
Outputs:
- next_pop: float32 [56, 4, 128, 1024], P('sec', None, 'gy', 'gz')
- pop_grad: float32 [56, 4, 128, 1024], P('sec', None, 'gy', 'gz')
- rate_grad: float32 [19], replicated
Inputs may be any that keep to these rules, and one draw needn't show every extreme that they name: `populations`: entries are positive.
All inputs are finite; a program needn't handle non-finite values. No bound on the sum of `solid_mask` on one device may be relied on, other than what follows from the above.
Results may differ from a plain program's by a relative error of at most 0.0003.
Values sent between devices are 32-bit elements; how exact they have to be, the bound alone decides.
No kernel may reach another device: no remote copies, remote signals or barrier semaphores. Data moves between devices by JAX's collectives and lax.ppermute only.
A program may use at most 64 MiB of HBM per device.

v0:
```python
from functools import partial
import jax
import jax.numpy as jnp
import numpy as np
from jax import lax
from jax.sharding import PartitionSpec as P


def extended(block, sides, width):
    for axis, dim in sides:
        count = lax.axis_size(axis)
        forward = [(i, i + 1) for i in range(count - 1)]
        forward.append((count - 1, 0))
        backward = [(target, source) for source, target in forward]
        low = lax.ppermute(
            lax.slice_in_dim(block, block.shape[dim] - width, None, axis=dim), axis, forward
        )
        high = lax.ppermute(lax.slice_in_dim(block, 0, width, axis=dim), axis, backward)
        block = jnp.concatenate([low, block, high], axis=dim)
    return block


def spread(shard, axis, root):
    mine = lax.axis_index(axis) == root
    return lax.psum(jnp.where(mine, shard, jnp.zeros_like(shard)), axis)


def orthonormal_columns(basis):
    result = []
    for column in range(basis.shape[1]):
        vector = basis[:, column] * 1.0
        for repeat in range(2):
            for earlier in result:
                vector = vector - np.sum(earlier * vector) * earlier
        vector = vector / np.sqrt(np.sum(vector * vector))
        result.append(vector)
    return np.stack(result, 1)


def lattice_tables():
    axis_moves = [(1, 0, 0), (-1, 0, 0), (0, 1, 0), (0, -1, 0), (0, 0, 1), (0, 0, -1)]
    edge_moves = []
    for first, second in ((0, 1), (0, 2), (1, 2)):
        for sign_first in (1, -1):
            for sign_second in (1, -1):
                move = [0, 0, 0]
                move[first] = sign_first
                move[second] = sign_second
                edge_moves.append(tuple(move))
    velocity = np.array([(0, 0, 0)] + axis_moves + edge_moves) * 1.0
    weights = np.array([1.0 / 3.0] + [1.0 / 18.0] * 6 + [1.0 / 36.0] * 12)
    opposite = np.array(
        [int(np.argmin(np.abs(velocity + velocity[channel]).sum(1))) for channel in range(19)]
    )
    along_x = velocity[:, 0]
    along_y = velocity[:, 1]
    along_z = velocity[:, 2]
    basis = np.stack(
        [
            np.ones(19),
            along_x,
            along_y,
            along_z,
            along_x**2,
            along_y**2,
            along_z**2,
            along_x * along_y,
            along_y * along_z,
            along_x * along_z,
            along_x * along_y**2,
            along_x * along_z**2,
            along_y * along_x**2,
            along_y * along_z**2,
            along_z * along_x**2,
            along_z * along_y**2,
            along_x**2 * along_y**2,
            along_x**2 * along_z**2,
            along_y**2 * along_z**2,
        ],
        1,
    )
    ortho = orthonormal_columns(basis)
    return (velocity, weights, opposite, ortho)


def expand(table, trailing):
    return jnp.asarray(table, jnp.float32).reshape(table.shape + (1,) * trailing)


def same_move(first_move, second_move):
    return tuple((int(value) for value in first_move)) == tuple(
        (int(value) for value in second_move)
    )


def flow_branch(is_fluid, rows, motion, flow_rates, species_rates):
    velocity, weights, opposite, ortho = lattice_tables()
    highest = lax.Precision.HIGHEST
    flow = rows[:19]
    trailing = flow.ndim - 1
    rates = jnp.concatenate([jnp.zeros((4,), flow_rates.dtype), flow_rates])
    ortho_table = jnp.asarray(ortho, jnp.float32)
    collision = jnp.dot(ortho_table * rates[None, :], ortho_table.T, precision=highest)
    velocity_table = jnp.asarray(velocity, jnp.float32)
    density = jnp.sum(flow, 0)
    projected = jnp.tensordot(velocity_table, motion, 1, precision=highest)
    squared = jnp.sum(motion * motion, 0)
    equilibrium = (
        expand(weights, trailing)
        * density
        * (1.0 + 3.0 * projected + 4.5 * projected * projected - 1.5 * squared)
    )
    relaxed = flow - jnp.tensordot(collision, flow - equilibrium, 1, precision=highest)
    flow_out = jnp.where(is_fluid, relaxed, flow[opposite])
    filler = jnp.zeros((rows.shape[0] - 19,) + rows.shape[1:], jnp.float32)
    return jnp.concatenate([flow_out, filler])


def species_branch(is_fluid, rows, motion, flow_rates, species_rates):
    velocity, weights, opposite, ortho = lattice_tables()
    highest = lax.Precision.HIGHEST
    trailing = rows.ndim - 1
    velocity_table = jnp.asarray(velocity[:7], jnp.float32)
    projected = jnp.tensordot(velocity_table, motion, 1, precision=highest)
    grouped = rows.reshape((rows.shape[0] // 7, 7) + rows.shape[1:])
    concentration = jnp.sum(grouped, 1)
    small_weights = np.array([0.25] + [0.125] * 6)
    species_eq = (
        expand(small_weights, trailing)[None]
        * concentration[:, None]
        * (1.0 + 4.0 * projected)[None]
    )
    rate_shape = species_rates.reshape((-1, 1) + (1,) * trailing)
    relaxed_species = grouped - rate_shape * (grouped - species_eq)
    return jnp.where(is_fluid, relaxed_species, grouped[:, opposite[:7]]).reshape(rows.shape)


def take_piece(padded, channel, move, size_y, size_z):
    step_x, step_y, step_z = (int(value) for value in move)
    piece = padded[channel, :, 1 - step_y : 1 - step_y + size_y, 1 - step_z : 1 - step_z + size_z]
    return jnp.roll(piece, step_x, 0)


def stream(field, table_flow, table_species, is_flow):
    padded = extended(field, (("gy", 2), ("gz", 3)), 1)
    size_y, size_z = (field.shape[2], field.shape[3])
    pieces = []
    for channel in range(field.shape[0]):
        first = take_piece(padded, channel, table_flow[channel], size_y, size_z)
        if same_move(table_flow[channel], table_species[channel]):
            pieces.append(first)
        else:
            second = take_piece(padded, channel, table_species[channel], size_y, size_z)
            pieces.append(jnp.where(is_flow, first, second))
    return jnp.stack(pieces)


def per_device(populations, solid_mask, flow_rates, species_rates, cotangents):
    velocity, weights, opposite, ortho = lattice_tables()
    highest = lax.Precision.HIGHEST
    rows_count = populations.shape[0]
    is_flow = lax.axis_index("sec") == 0
    is_fluid = solid_mask == 0
    velocity_table = jnp.asarray(velocity, jnp.float32)
    density = jnp.sum(populations[:19], 0)
    own_motion = jnp.tensordot(velocity_table.T, populations[:19], 1, precision=highest) / density
    motion = spread(own_motion, "sec", 0)

    def forward(rows, shared, rates_a, rates_b):
        return lax.cond(
            is_flow,
            partial(flow_branch, is_fluid),
            partial(species_branch, is_fluid),
            rows,
            shared,
            rates_a,
            rates_b,
        )

    post, pullback = jax.vjp(forward, populations, motion, flow_rates, species_rates)
    table_flow = np.concatenate([velocity, np.zeros((rows_count - 19, 3))])
    table_species = np.tile(velocity[:7], (rows_count // 7, 1))
    returned = stream(cotangents, -table_flow, -table_species, is_flow)
    moved = stream(post, table_flow, table_species, is_flow)
    grad_rows, grad_motion, local_flow_rates, local_species_rates = pullback(returned)
    from_species = spread(grad_motion, "sec", 1)
    total_motion = grad_motion + from_species
    along = jnp.tensordot(velocity_table, total_motion, 1, precision=highest)
    extra = (along - jnp.sum(own_motion * total_motion, 0)[None]) / density[None]
    filler = jnp.zeros((rows_count - 19,) + populations.shape[1:], jnp.float32)
    grad_rows = grad_rows + jnp.where(is_flow, jnp.concatenate([extra, filler]), 0.0)
    summed_flow_rates, summed_species_rates = lax.psum(
        (local_flow_rates, local_species_rates), ("sec", "gy", "gz")
    )
    rate_grad = jnp.concatenate([summed_flow_rates, summed_species_rates])
    return (moved, grad_rows, rate_grad)


def solution(mesh):
    placed = (P("sec", None, "gy", "gz"), P(None, "gy", "gz"), P(), P(), P("sec", None, "gy", "gz"))
    return jax.shard_map(
        per_device,
        mesh=mesh,
        in_specs=placed,
        out_specs=(P("sec", None, "gy", "gz"), P("sec", None, "gy", "gz"), P()),
        check_vma=False,
    )
```

profile of v0, /device:TPU:1, one launch (start us, length us, event | category | flops | bytes accessed | tf_op | source)
XLA Modules:
  0.0 205.7 jit_solution(12356524541416200816)
XLA Ops:
  0.6 0.7 broadcast_compare_fusion
  1.4 1.0 slice_reduce_fusion.1
  2.4 1.1 broadcast_select_fusion.4
  3.5 10.7 %psum.28 = f32[3,4,8,128]{3,0,2,1:T(4,128)S(1)} all-reduce(f32[3,4,8,128]{3,0,2,1:T(4,128)S(1)} %get-tuple-element.572), channel_id=1, replica_groups=mesh['sec'=2,'gy'=16,'gz'=8] {'sec'}, use_global_device_ids=true, to_apply=%region_1.2 | all-reduce | flops 12288 | bytes 98304 | tf_op jit(solution)/shard_map/psum | solution.py:25
  14.9 8.5 %conditional.2 = (f32[28,4,8,128]{3,0,2,1:T(8,128)S(1)}, f32[7,3]{1,0:T(8,128)S(1)}, f32[1,7,1,1,1]{4,3,2,1,0:T(1,128)S(1)}, f32[1,7,4,8,128]{4,3,2,1,0:T(8,128)...) conditional(s32[]{:T(128)} %convert_element_type.3, ...), branch_computations={%region_2.4_spmd.clone, %region_4.7_spmd.clone} | conditional | flops 21583616 | bytes 10085426 | solution.py:170
  16.0 1.6 multiply_subtract_fusion.1
  21.1 0.7 copy-done.68
  28.3 2.9 %collective-permute-start = (f32[28,4,1,128]{3,2,1,0:T(1,128)}, f32[28,4,1,128]{3,2,1,0:T(1,128)S(1)}, u32[]{:S(2)}, u32[]{:S(2)}) collective-permute-start(f32[28,4,1,128]{3,2,1,0:T(1,128)} %copy.353), channel_id=1, source_target_pairs={{0,8},{8,16},{16,24},{24,32},{32,40},{40,48},{48,56},{56,64},{64,7... | collective-permute-start | bytes 172040 | tf_op jit(solution)/shard_map/ppermute | solution.py:15
  31.8 0.7 fusion.71
  32.6 3.8 %collective-permute-start.4 = (f32[28,4,1,128]{3,2,1,0:T(1,128)}, f32[28,4,1,128]{3,2,1,0:T(1,128)S(1)}, u32[]{:S(2)}, u32[]{:S(2)}) collective-permute-start(f32[28,4,1,128]{3,2,1,0:T(1,128)} %get-tuple-element.553), channel_id=1, source_target_pairs={{8,0},{16,8},{24,16},{32,24},{40,32},{48,40},{56,48},{64,56},{72,6... | collective-permute-start | bytes 172040 | tf_op jit(solution)/shard_map/ppermute | solution.py:18
  36.4 1.1 constant_dynamic-update-slice_fusion
  40.6 0.8 constant_dynamic-update-slice_fusion.29
  42.6 2.8 %dynamic-update-slice.59 = f32[28,4,9,128]{3,2,1,0:T(8,128)} dynamic-update-slice(f32[28,4,9,128]{3,2,1,0:T(8,128)} %get-tuple-element.508, f32[28,4,1,128]{3,2,1,0:T(1,128)S(1)} %collective-permute-done.1, s32[]{} %constant.121, s32[]{} %constant.121, s32[]{} %constant.129, s32[]{} %constant.121) | dynamic-update-slice | bytes 114692 | tf_op jit(solution)/shard_map/concatenate | solution.py:19
  45.4 1.4 fusion.65
  47.4 1.4 constant_dynamic-update-slice_fusion.24
  49.3 1.3 fusion.66
  50.6 2.8 %dynamic-update-slice.29 = f32[28,4,9,128]{3,2,1,0:T(8,128)} dynamic-update-slice(f32[28,4,9,128]{3,2,1,0:T(8,128)} %constant_dynamic-update-slice_fusion.29, f32[28,4,1,128]{3,2,1,0:T(1,128)S(1)} %collective-permute-done.4, s32[]{} %constant.121, s32[]{} %constant.121, s32[]{} %constant.129, s32[]{} %constant.121) | dynamic-update-slice | bytes 114692 | tf_op jit(solution)/shard_map/concatenate | solution.py:19
  53.4 1.4 fusion.63
  54.7 0.8 constant_dynamic-update-slice_fusion.54
  55.5 1.3 fusion.62
  56.8 1.3 copy.358
  58.0 1.5 collective-permute-start.2
  59.5 1.3 copy.360
  60.8 3.9 %collective-permute-start.3 = (f32[28,4,10,1]{0,2,3,1:T(8,128)}, f32[28,4,10,1]{0,2,3,1:T(8,128)}, u32[]{:S(2)}, u32[]{:S(2)}) collective-permute-start(f32[28,4,10,1]{0,2,3,1:T(8,128)} %copy.360), channel_id=1, source_target_pairs={{1,0},{2,1},{3,2},{4,3},{5,4},{6,5},{7,6},{0,7},{9,8},{10,9},{11,1... | collective-permute-start | bytes 13448 | tf_op jit(solution)/shard_map/ppermute | solution.py:18
  65.2 1.3 copy.385
  66.5 1.5 collective-permute-start.6
  68.0 1.3 copy.387
  69.2 1.7 copy.359
  70.9 1.7 copy.361
  77.3 1.4 constant_dynamic-update-slice_fusion.17
  83.0 1.4 constant_dynamic-update-slice_fusion.10
  88.4 1.4 constant_dynamic-update-slice_fusion.3
  89.8 2.5 %copy.386 = f32[28,4,10,1]{3,2,1,0:T(8,128)} copy(f32[28,4,10,1]{0,2,3,1:T(8,128)} %collective-permute-done.6) | data formatting | bytes 8960 | tf_op jit(solution)/shard_map/ppermute | solution.py:18
  92.3 2.5 %copy.388 = f32[28,4,10,1]{3,2,1,0:T(8,128)} copy(f32[28,4,10,1]{0,2,3,1:T(8,128)} %collective-permute-done.7) | data formatting | bytes 8960 | tf_op jit(solution)/shard_map/ppermute | solution.py:15
  94.8 0.9 constant_dynamic-update-slice_fusion.52
  96.8 0.8 constant_dynamic-update-slice_fusion.47
  99.4 0.8 constant_dynamic-update-slice_fusion.40
  101.8 0.8 constant_dynamic-update-slice_fusion.33
  103.5 9.2 %conditional.3 = (f32[3,4,8,128]{3,0,2,1:T(4,128)S(1)}, f32[15]{0:T(128)S(1)}, f32[4]{0:T(128)S(1)}, f32[28,4,8,128]{3,0,2,1:T(8,128)}) conditional(s32[]{:T(128)} %convert_element_type.3, (f32[28,4,8,128]{3,2,1,0:T(8,128)S(1)}, pred[4,7,4,8,128]{4,3,2,1,0:T(8,128)(4,1)}, f32[4,1,1,1,1]{4,3,2,1,0:T(1,128)S(1)}, f32[1,7,1,1,1]{4,3,2,1,0:T(1,128)}, ...), branch_computations={%region_7.12_spmd, %region_12.17_spmd} | conditional | flops 40199236 | bytes 13603772 | solution.py:170
  103.9 0.7 copy-done.7
  104.6 1.7 multiply_reduce_fusion.4
  106.4 1.5 fusion.15
  109.7 1.9 scatter_fusion.1
  111.8 0.9 pad.5.clone
  113.3 8.1 %psum.29 = f32[3,4,8,128]{3,0,2,1:T(4,128)S(1)} all-reduce(f32[3,4,8,128]{3,0,2,1:T(4,128)S(1)} %broadcast_select_fusion.3), channel_id=1, replica_groups=mesh['sec'=2,'gy'=16,'gz'=8] {'sec'}, use_global_device_ids=true, to_apply=%region_17.18 | all-reduce | flops 12288 | bytes 98304 | tf_op jit(solution)/shard_map/psum | solution.py:25
  122.6 1.1 select_add_fusion
  123.7 1.0 copy.398
  125.4 78.3 %all-reduce.4 = (f32[4]{0:T(128)S(1)}, f32[15]{0:T(128)S(1)}) all-reduce(f32[4]{0:T(128)S(1)} %get-tuple-element.174, f32[15]{0:T(128)S(1)} %copy-done.85), channel_id=1, replica_groups=mesh['sec'=2,'gy'=16,'gz'=8] {'sec','gy','gz'}, use_global_device_ids=true, to_apply=%region_20.21 | all-reduce | flops 19 | bytes 152 | tf_op jit(solution)/shard_map/psum | solution.py:192
  (264 shorter events, 42.9 us)
Async XLA Ops:
  1.4 1.0 copy-start.86
  2.4 1.2 copy-start.49
  2.4 11.9 %copy-start.3 = (f32[28,4,8,128]{3,2,1,0:T(8,128)S(1)}, f32[28,4,8,128]{3,2,1,0:T(8,128)}, u32[]{:S(2)}) copy-start(f32[28,4,8,128]{3,2,1,0:T(8,128)} %param.19) | copy-start | bytes 1376260
  14.9 4.4 %copy-start.8 = (pred[19,4,8,128]{3,0,2,1:T(8,128)(4,1)}, pred[19,4,8,128]{3,0,2,1:T(8,128)(4,1)S(1)}, u32[]{:S(2)}) copy-start(pred[19,4,8,128]{3,0,2,1:T(8,128)(4,1)S(1)} %broadcast_in_dim.48) | copy-start | bytes 233476 | tf_op jit(solution)/shard_map/jvp()/cond
  17.6 1.8 copy-start.4
  17.7 0.8 copy-start.80
  21.1 0.7 copy-start.68
  22.5 0.9 copy-start.9
  22.6 0.9 copy-start.17
  27.0 4.8 %copy-start.12 = (f32[3,4,8,128]{3,0,2,1:T(4,128)}, f32[3,4,8,128]{3,0,2,1:T(4,128)S(1)}, u32[]{:S(2)}) copy-start(f32[3,4,8,128]{3,0,2,1:T(4,128)S(1)} %get-tuple-element.164) | copy-start | bytes 147460
  27.0 10.5 %copy-start.6 = (f32[19,4,8,128]{3,0,2,1:T(8,128)}, f32[19,4,8,128]{3,0,2,1:T(8,128)S(1)}, u32[]{:S(2)}) copy-start(f32[19,4,8,128]{3,0,2,1:T(8,128)S(1)} %get-tuple-element.163) | copy-start | bytes 933892
  27.0 10.5 %copy-start.10 = (f32[4,7,4,8,128]{4,3,2,1,0:T(8,128)}, f32[4,7,4,8,128]{4,3,2,1,0:T(8,128)S(1)}, u32[]{:S(2)}) copy-start(f32[4,7,4,8,128]{4,3,2,1,0:T(8,128)S(1)} %get-tuple-element.157) | copy-start | bytes 1376260
  27.0 10.5 %copy-start.11 = (f32[4,7,4,8,128]{4,3,2,1,0:T(8,128)}, f32[4,7,4,8,128]{4,3,2,1,0:T(8,128)S(1)}, u32[]{:S(2)}) copy-start(f32[4,7,4,8,128]{4,3,2,1,0:T(8,128)S(1)} %get-tuple-element.155) | copy-start | bytes 1376260
  27.0 10.4 %copy-start.14 = (f32[19,4,8,128]{3,0,2,1:T(8,128)}, f32[19,4,8,128]{3,0,2,1:T(8,128)S(1)}, u32[]{:S(2)}) copy-start(f32[19,4,8,128]{3,0,2,1:T(8,128)S(1)} %get-tuple-element.166) | copy-start | bytes 933892
  27.0 4.8 %copy-start = (f32[28,4,8,128]{3,2,1,0:T(8,128)S(1)}, f32[28,4,8,128]{3,2,1,0:T(8,128)}, u32[]{:S(2)}) copy-start(f32[28,4,8,128]{3,2,1,0:T(8,128)} %param.23) | copy-start | bytes 1376260
  28.3 18.5 %collective-permute-start = (f32[28,4,1,128]{3,2,1,0:T(1,128)}, f32[28,4,1,128]{3,2,1,0:T(1,128)S(1)}, u32[]{:S(2)}, u32[]{:S(2)}) collective-permute-start(f32[28,4,1,128]{3,2,1,0:T(1,128)} %copy.353), channel_id=1, source_target_pairs={{0,8},{8,16},{16,24},{24,32},{32,40},{40,48},{48,56},{56,64},{64,7... | collective-permute-start | bytes 172040 | tf_op jit(solution)/shard_map/ppermute | solution.py:15
  31.8 10.8 %collective-permute-start.1 = (f32[28,4,1,128]{3,2,1,0:T(1,128)}, f32[28,4,1,128]{3,2,1,0:T(1,128)S(1)}, u32[]{:S(2)}, u32[]{:S(2)}) collective-permute-start(f32[28,4,1,128]{3,2,1,0:T(1,128)} %copy.355), channel_id=1, source_target_pairs={{8,0},{16,8},{24,16},{32,24},{40,32},{48,40},{56,48},{64,56},{72,6... | collective-permute-start | bytes 172040 | tf_op jit(solution)/shard_map/ppermute | solution.py:18
  32.6 18.0 %collective-permute-start.4 = (f32[28,4,1,128]{3,2,1,0:T(1,128)}, f32[28,4,1,128]{3,2,1,0:T(1,128)S(1)}, u32[]{:S(2)}, u32[]{:S(2)}) collective-permute-start(f32[28,4,1,128]{3,2,1,0:T(1,128)} %get-tuple-element.553), channel_id=1, source_target_pairs={{8,0},{16,8},{24,16},{32,24},{40,32},{48,40},{56,48},{64,56},{72,6... | collective-permute-start | bytes 172040 | tf_op jit(solution)/shard_map/ppermute | solution.py:18
  36.4 28.4 %collective-permute-start.5 = (f32[28,4,1,128]{3,2,1,0:T(1,128)}, f32[28,4,1,128]{3,2,1,0:T(1,128)S(1)}, u32[]{:S(2)}, u32[]{:S(2)}) collective-permute-start(f32[28,4,1,128]{3,2,1,0:T(1,128)} %get-tuple-element.552), channel_id=1, source_target_pairs={{0,8},{8,16},{16,24},{24,32},{32,40},{40,48},{48,56},{56,64},{64,7... | collective-permute-start | bytes 172040 | tf_op jit(solution)/shard_map/ppermute | solution.py:15
  58.0 11.2 %collective-permute-start.2 = (f32[28,4,10,1]{0,2,3,1:T(8,128)}, f32[28,4,10,1]{0,2,3,1:T(8,128)}, u32[]{:S(2)}, u32[]{:S(2)}) collective-permute-start(f32[28,4,10,1]{0,2,3,1:T(8,128)} %copy.358), channel_id=1, source_target_pairs={{0,1},{1,2},{2,3},{3,4},{4,5},{5,6},{6,7},{7,0},{8,9},{9,10},{10,1... | collective-permute-start | bytes 13448 | tf_op jit(solution)/shard_map/ppermute | solution.py:15
  60.8 10.1 %collective-permute-start.3 = (f32[28,4,10,1]{0,2,3,1:T(8,128)}, f32[28,4,10,1]{0,2,3,1:T(8,128)}, u32[]{:S(2)}, u32[]{:S(2)}) collective-permute-start(f32[28,4,10,1]{0,2,3,1:T(8,128)} %copy.360), channel_id=1, source_target_pairs={{1,0},{2,1},{3,2},{4,3},{5,4},{6,5},{7,6},{0,7},{9,8},{10,9},{11,1... | collective-permute-start | bytes 13448 | tf_op jit(solution)/shard_map/ppermute | solution.py:18
  66.5 23.3 %collective-permute-start.6 = (f32[28,4,10,1]{0,2,3,1:T(8,128)}, f32[28,4,10,1]{0,2,3,1:T(8,128)}, u32[]{:S(2)}, u32[]{:S(2)}) collective-permute-start(f32[28,4,10,1]{0,2,3,1:T(8,128)} %copy.385), channel_id=1, source_target_pairs={{1,0},{2,1},{3,2},{4,3},{5,4},{6,5},{7,6},{0,7},{9,8},{10,9},{11,1... | collective-permute-start | bytes 13448 | tf_op jit(solution)/shard_map/ppermute | solution.py:18
  69.2 23.1 %collective-permute-start.7 = (f32[28,4,10,1]{0,2,3,1:T(8,128)}, f32[28,4,10,1]{0,2,3,1:T(8,128)}, u32[]{:S(2)}, u32[]{:S(2)}) collective-permute-start(f32[28,4,10,1]{0,2,3,1:T(8,128)} %copy.387), channel_id=1, source_target_pairs={{0,1},{1,2},{2,3},{3,4},{4,5},{5,6},{6,7},{7,0},{8,9},{9,10},{10,1... | collective-permute-start | bytes 13448 | tf_op jit(solution)/shard_map/ppermute | solution.py:15
  74.0 0.7 copy-start.35
  74.0 0.7 copy-start.63
  75.3 0.7 copy-start.37
  75.3 0.7 copy-start.47
  85.1 2.0 copy-start.28
  85.8 0.7 copy-start.55
  94.8 1.2 copy-start.2
  96.0 0.7 copy-start.36
  96.0 0.7 copy-start.44
  96.0 0.7 copy-start.27
  96.0 0.7 copy-start.33
  96.0 0.7 copy-start.53
  96.0 0.7 copy-start.61
  96.1 1.4 copy-start.1
  100.4 0.8 copy-start.25
  100.4 0.7 copy-start.26
  100.4 0.7 copy-start.52
  102.8 0.7 copy-start.19
  102.8 0.7 copy-start.40
  103.6 1.0 copy-start.7
  104.6 1.7 copy-start.13
  104.6 1.8 copy-start.15
  106.4 1.6 copy-start.5
  113.2 8.1 %copy-start.20 = (f32[3,4,8,128]{3,0,2,1:T(4,128)S(1)}, f32[3,4,8,128]{3,0,2,1:T(4,128)}, u32[]{:S(2)}) copy-start(f32[3,4,8,128]{3,0,2,1:T(4,128)} %get-tuple-element.573) | copy-start | bytes 147460
  121.4 0.7 copy-start.50
  (39 other events, 26.1 us)
where the time goes:
time: 208 us; the launch traced here: 206 us
  blocking collectives  97.1 us (47%)
  local copies, waits for them, and re-layouts  56.7 us (27%)
  other arithmetic  29 us (14%)
  starting transfers between devices  13.6 us (7%)
  matrix products  7.89 us (4%)
    psum x1, blocking collectives, per_device(): lax.psum((local_flow_rates, local_species_rates), ('sec', 'gy', 'gz'))  78.3 us
    unnamed x48, other arithmetic  22.2 us
    psum x2, blocking collectives, spread(): return lax.psum(jnp.where(mine, shard, jnp.zeros_like(shard)), axis)  18.8 us
    unnamed x131, local copies, waits for them, and re-layouts  18.2 us
    ppermute x4, starting transfers between devices, extended(): lax.ppermute(lax.slice_in_dim(block, 0, width, axis=dim), axis, backward)  9.2 us
    slice x8, local copies, waits for them, and re-layouts, take_piece(): return jnp.roll(piece, step_x, 0)  7.86 us
    concatenate x2, local copies, waits for them, and re-layouts, extended(): block = jnp.concatenate([low, block, high], axis=dim)  5.54 us
    cond x40, local copies, waits for them, and re-layouts  5.1 us
  transfers between devices with their start and end apart: 8, of which 0 were waited for; matrix products, arithmetic and copies ran while one was open for 24% of the time, Pallas kernels for 0%

commit v1 on v0

--- a/solution.py
+++ b/solution.py
@@ -189,8 +189,14 @@
     extra = (along - jnp.sum(own_motion * total_motion, 0)[None]) / density[None]
     filler = jnp.zeros((rows_count - 19,) + populations.shape[1:], jnp.float32)
     grad_rows = grad_rows + jnp.where(is_flow, jnp.concatenate([extra, filler]), 0.0)
-    summed_flow_rates, summed_species_rates = lax.psum(
-        (local_flow_rates, local_species_rates), ("sec", "gy", "gz")
+
+    def pass_cards_on(x0, group_axis, link_axis):
+        for at in (group_axis, link_axis):
+            x0 = lax.psum(x0, axis_name=at)
+        return x0
+
+    summed_flow_rates, summed_species_rates = pass_cards_on(
+        (local_flow_rates, local_species_rates), "sec", ("gy", "gz")
     )
     rate_grad = jnp.concatenate([summed_flow_rates, summed_species_rates])
     return (moved, grad_rows, rate_grad)

time: 208 us -> 410 us (1.97)
  the two profiles are of different devices: /device:TPU:1 before, /device:TPU:4 now
where the time goes in v1:
time: 410 us; the launch traced here: 408 us
  blocking collectives  302 us (74%)
  local copies, waits for them, and re-layouts  59.5 us (15%)
  other arithmetic  31.9 us (8%)
  starting transfers between devices  10.8 us (3%)
    psum x1, blocking collectives, pass_cards_on(): x0 = lax.psum(x0, axis_name=at)  279 us
    psum x2, blocking collectives, spread(): return lax.psum(jnp.where(mine, shard, jnp.zeros_like(shard)), axis)  22.9 us
    unnamed x48, other arithmetic  22.2 us
    unnamed x129, local copies, waits for them, and re-layouts  17.5 us
    ppermute x4, starting transfers between devices, extended(): lax.ppermute(lax.slice_in_dim(block, 0, width, axis=dim), axis, backward)  9.82 us
  transfers between devices with their start and end apart: 8, of which 0 were waited for; matrix products, arithmetic and copies ran while one was open for 12% of the time, Pallas kernels for 0%

profile of v1, /device:TPU:4, one launch (start us, length us, event | category | flops | bytes accessed | tf_op | source)
XLA Modules:
  0.0 408.1 jit_solution(9388792397319141078)
XLA Ops:
  0.6 0.7 broadcast_compare_fusion
  1.4 1.0 slice_reduce_fusion.1
  2.4 1.1 broadcast_select_fusion.4
  3.5 11.1 %psum.42 = f32[3,4,8,128]{3,0,2,1:T(4,128)S(1)} all-reduce(f32[3,4,8,128]{3,0,2,1:T(4,128)S(1)} %get-tuple-element.575), channel_id=1, replica_groups=mesh['sec'=2,'gy'=16,'gz'=8] {'sec'}, use_global_device_ids=true, to_apply=%region_1.2 | all-reduce | flops 12288 | bytes 98304 | tf_op jit(solution)/shard_map/psum | solution.py:25
  15.3 9.5 %conditional.2 = (f32[28,4,8,128]{3,0,2,1:T(8,128)S(1)}, f32[7,3]{1,0:T(8,128)S(1)}, f32[1,7,1,1,1]{4,3,2,1,0:T(1,128)S(1)}, f32[1,7,4,8,128]{4,3,2,1,0:T(8,128)...) conditional(s32[]{:T(128)} %convert_element_type.3, ...), branch_computations={%region_2.4_spmd.clone, %region_4.7_spmd.clone} | conditional | flops 21583616 | bytes 10085426 | solution.py:170
  21.8 0.8 broadcast.204.clone
  22.6 0.8 broadcast.204.clone.1
  23.4 0.8 broadcast.204.clone.3
  30.3 3.9 collective-permute-start.1
  34.2 0.7 fusion.71
  35.4 1.1 constant_dynamic-update-slice_fusion
  39.6 0.8 constant_dynamic-update-slice_fusion.29
  41.7 2.8 dynamic-update-slice.59
  44.5 1.4 fusion.65
  46.4 1.4 constant_dynamic-update-slice_fusion.24
  48.3 1.3 fusion.66
  49.6 2.8 dynamic-update-slice.29
  52.4 1.4 fusion.63
  53.7 0.8 constant_dynamic-update-slice_fusion.54
  54.5 1.3 fusion.62
  55.8 1.3 copy.358
  57.6 1.3 copy.360
  58.8 3.9 collective-permute-start.3
  63.3 1.3 copy.385
  64.5 2.0 collective-permute-start.6
  66.6 1.3 copy.387
  67.8 1.7 copy.359
  69.5 1.7 copy.361
  75.9 1.4 constant_dynamic-update-slice_fusion.17
  77.4 0.7 constant_dynamic-update-slice_fusion.16
  81.6 1.4 constant_dynamic-update-slice_fusion.10
  87.0 1.4 constant_dynamic-update-slice_fusion.3
  88.4 2.5 copy.386
  90.9 2.5 copy.388
  93.4 0.9 constant_dynamic-update-slice_fusion.52
  95.4 0.8 constant_dynamic-update-slice_fusion.47
  97.9 0.8 constant_dynamic-update-slice_fusion.40
  100.4 0.8 constant_dynamic-update-slice_fusion.33
  102.1 8.8 %conditional.3 = (f32[3,4,8,128]{3,0,2,1:T(4,128)S(1)}, f32[15]{0:T(128)S(1)}, f32[4]{0:T(128)S(1)}, f32[28,4,8,128]{3,0,2,1:T(8,128)}) conditional(s32[]{:T(128)} %convert_element_type.3, (f32[28,4,8,128]{3,2,1,0:T(8,128)S(1)}, pred[4,7,4,8,128]{4,3,2,1,0:T(8,128)(4,1)}, f32[4,1,1,1,1]{4,3,2,1,0:T(1,128)S(1)}, f32[1,7,1,1,1]{4,3,2,1,0:T(1,128)}, ...), branch_computations={%region_7.12_spmd, %region_12.17_spmd} | conditional | flops 40199236 | bytes 13603772 | solution.py:170
  103.0 1.5 multiply_reduce_fusion.3
  105.5 1.8 select_bitcast_fusion
  107.4 1.0 copy.342
  108.5 1.3 scatter_fusion
  109.8 1.1 copy.410
  111.5 11.8 %all-reduce.5 = (f32[3,4,8,128]{3,0,2,1:T(4,128)S(1)}, f32[4]{0:T(128)S(1)}, f32[15]{0:T(128)S(1)}) all-reduce(f32[3,4,8,128]{3,0,2,1:T(4,128)S(1)} %broadcast_select_fusion.3, f32[4]{0:T(128)S(1)} %get-tuple-element.174, f32[15]{0:T(128)} %copy-done.79), channel_id=1, replica_groups=mesh['sec'=2,'gy'=16,'gz'=8] {'sec'}, use_global_device_ids=true, to_apply=%region_17.18 | all-reduce | flops 12307 | bytes 98456 | tf_op jit(solution)/shard_map/psum | solution.py:25
  124.5 1.1 select_add_fusion
  125.6 1.0 copy.398
  126.7 279.5 %all-reduce.4 = (f32[4]{0:T(128)S(1)}, f32[15]{0:T(128)S(1)}) all-reduce(f32[4]{0:T(128)S(1)} %get-tuple-element.503, f32[15]{0:T(128)S(1)} %get-tuple-element.504), channel_id=1, replica_groups=mesh['sec'=2,'gy'=16,'gz'=8] {'gy','gz'}, use_global_device_ids=true, to_apply=%region_22.23 | all-reduce | flops 19 | bytes 152 | tf_op jit(solution)/shard_map/psum | solution.py:195
  (248 shorter events, 43.2 us)
Async XLA Ops:
  1.4 1.0 copy-start.85
  2.4 1.2 copy-start.49
  2.4 12.3 %copy-start.3 = (f32[28,4,8,128]{3,2,1,0:T(8,128)S(1)}, f32[28,4,8,128]{3,2,1,0:T(8,128)}, u32[]{:S(2)}) copy-start(f32[28,4,8,128]{3,2,1,0:T(8,128)} %param.19) | copy-start | bytes 1376260
  28.4 2.0 copy-start.12
  28.4 8.1 %copy-start.6 = (f32[19,4,8,128]{3,0,2,1:T(8,128)}, f32[19,4,8,128]{3,0,2,1:T(8,128)S(1)}, u32[]{:S(2)}) copy-start(f32[19,4,8,128]{3,0,2,1:T(8,128)S(1)} %get-tuple-element.163) | copy-start | bytes 933892
  28.4 8.1 %copy-start.10 = (f32[4,7,4,8,128]{4,3,2,1,0:T(8,128)}, f32[4,7,4,8,128]{4,3,2,1,0:T(8,128)S(1)}, u32[]{:S(2)}) copy-start(f32[4,7,4,8,128]{4,3,2,1,0:T(8,128)S(1)} %get-tuple-element.157) | copy-start | bytes 1376260
  28.4 8.1 %copy-start.11 = (f32[4,7,4,8,128]{4,3,2,1,0:T(8,128)}, f32[4,7,4,8,128]{4,3,2,1,0:T(8,128)S(1)}, u32[]{:S(2)}) copy-start(f32[4,7,4,8,128]{4,3,2,1,0:T(8,128)S(1)} %get-tuple-element.155) | copy-start | bytes 1376260
  28.4 8.1 %copy-start.14 = (f32[19,4,8,128]{3,0,2,1:T(8,128)}, f32[19,4,8,128]{3,0,2,1:T(8,128)S(1)}, u32[]{:S(2)}) copy-start(f32[19,4,8,128]{3,0,2,1:T(8,128)S(1)} %get-tuple-element.166) | copy-start | bytes 933892
  28.4 5.8 %copy-start = (f32[28,4,8,128]{3,2,1,0:T(8,128)S(1)}, f32[28,4,8,128]{3,2,1,0:T(8,128)}, u32[]{:S(2)}) copy-start(f32[28,4,8,128]{3,2,1,0:T(8,128)} %param.23) | copy-start | bytes 1376260
  29.6 16.2 %collective-permute-start = (f32[28,4,1,128]{3,2,1,0:T(1,128)}, f32[28,4,1,128]{3,2,1,0:T(1,128)S(1)}, u32[]{:S(2)}, u32[]{:S(2)}) collective-permute-start(f32[28,4,1,128]{3,2,1,0:T(1,128)} %copy.353), channel_id=1, source_target_pairs={{0,8},{8,16},{16,24},{24,32},{32,40},{40,48},{48,56},{56,64},{64,7... | collective-permute-start | bytes 172040 | tf_op jit(solution)/shard_map/ppermute | solution.py:15
  30.3 11.4 %collective-permute-start.1 = (f32[28,4,1,128]{3,2,1,0:T(1,128)}, f32[28,4,1,128]{3,2,1,0:T(1,128)S(1)}, u32[]{:S(2)}, u32[]{:S(2)}) collective-permute-start(f32[28,4,1,128]{3,2,1,0:T(1,128)} %copy.355), channel_id=1, source_target_pairs={{8,0},{16,8},{24,16},{32,24},{40,32},{48,40},{56,48},{64,56},{72,6... | collective-permute-start | bytes 172040 | tf_op jit(solution)/shard_map/ppermute | solution.py:18
  34.9 14.7 %collective-permute-start.4 = (f32[28,4,1,128]{3,2,1,0:T(1,128)}, f32[28,4,1,128]{3,2,1,0:T(1,128)S(1)}, u32[]{:S(2)}, u32[]{:S(2)}) collective-permute-start(f32[28,4,1,128]{3,2,1,0:T(1,128)} %get-tuple-element.556), channel_id=1, source_target_pairs={{8,0},{16,8},{24,16},{32,24},{40,32},{48,40},{56,48},{64,56},{72,6... | collective-permute-start | bytes 172040 | tf_op jit(solution)/shard_map/ppermute | solution.py:18
  34.9 27.9 %collective-permute-start.5 = (f32[28,4,1,128]{3,2,1,0:T(1,128)}, f32[28,4,1,128]{3,2,1,0:T(1,128)S(1)}, u32[]{:S(2)}, u32[]{:S(2)}) collective-permute-start(f32[28,4,1,128]{3,2,1,0:T(1,128)} %get-tuple-element.555), channel_id=1, source_target_pairs={{0,8},{8,16},{16,24},{24,32},{32,40},{40,48},{48,56},{56,64},{64,7... | collective-permute-start | bytes 172040 | tf_op jit(solution)/shard_map/ppermute | solution.py:15
  57.1 10.8 %collective-permute-start.2 = (f32[28,4,10,1]{0,2,3,1:T(8,128)}, f32[28,4,10,1]{0,2,3,1:T(8,128)}, u32[]{:S(2)}, u32[]{:S(2)}) collective-permute-start(f32[28,4,10,1]{0,2,3,1:T(8,128)} %copy.358), channel_id=1, source_target_pairs={{0,1},{1,2},{2,3},{3,4},{4,5},{5,6},{6,7},{7,0},{8,9},{9,10},{10,1... | collective-permute-start | bytes 13448 | tf_op jit(solution)/shard_map/ppermute | solution.py:15
  58.8 10.7 %collective-permute-start.3 = (f32[28,4,10,1]{0,2,3,1:T(8,128)}, f32[28,4,10,1]{0,2,3,1:T(8,128)}, u32[]{:S(2)}, u32[]{:S(2)}) collective-permute-start(f32[28,4,10,1]{0,2,3,1:T(8,128)} %copy.360), channel_id=1, source_target_pairs={{1,0},{2,1},{3,2},{4,3},{5,4},{6,5},{7,6},{0,7},{9,8},{10,9},{11,1... | collective-permute-start | bytes 13448 | tf_op jit(solution)/shard_map/ppermute | solution.py:18
  64.5 23.9 %collective-permute-start.6 = (f32[28,4,10,1]{0,2,3,1:T(8,128)}, f32[28,4,10,1]{0,2,3,1:T(8,128)}, u32[]{:S(2)}, u32[]{:S(2)}) collective-permute-start(f32[28,4,10,1]{0,2,3,1:T(8,128)} %copy.385), channel_id=1, source_target_pairs={{1,0},{2,1},{3,2},{4,3},{5,4},{6,5},{7,6},{0,7},{9,8},{10,9},{11,1... | collective-permute-start | bytes 13448 | tf_op jit(solution)/shard_map/ppermute | solution.py:18
  67.8 23.1 %collective-permute-start.7 = (f32[28,4,10,1]{0,2,3,1:T(8,128)}, f32[28,4,10,1]{0,2,3,1:T(8,128)}, u32[]{:S(2)}, u32[]{:S(2)}) collective-permute-start(f32[28,4,10,1]{0,2,3,1:T(8,128)} %copy.387), channel_id=1, source_target_pairs={{0,1},{1,2},{2,3},{3,4},{4,5},{5,6},{6,7},{7,0},{8,9},{9,10},{10,1... | collective-permute-start | bytes 13448 | tf_op jit(solution)/shard_map/ppermute | solution.py:15
  72.6 0.7 copy-start.35
  72.6 0.7 copy-start.63
  73.9 0.7 copy-start.37
  73.9 0.7 copy-start.47
  74.6 0.7 copy-start.38
  74.6 0.7 copy-start.48
  78.8 0.7 copy-start.46
  79.5 0.7 copy-start.45
  83.7 2.0 copy-start.28
  84.4 0.7 copy-start.29
  84.4 0.7 copy-start.55
  93.4 1.2 copy-start.2
  94.6 0.7 copy-start.62
  94.6 0.7 copy-start.36
  94.6 0.7 copy-start.44
  94.6 0.7 copy-start.27
  94.6 0.7 copy-start.33
  94.6 0.7 copy-start.53
  94.6 0.7 copy-start.61
  94.7 1.4 copy-start.1
  96.4 0.7 copy-start.22
  99.0 0.8 copy-start.25
  99.0 0.7 copy-start.26
  99.0 0.7 copy-start.52
  101.4 0.7 copy-start.19
  101.4 0.7 copy-start.40
  101.4 0.7 copy-start.70
  105.5 1.9 copy-start.60
  111.4 11.8 %copy-start.20 = (f32[3,4,8,128]{3,0,2,1:T(4,128)S(1)}, f32[3,4,8,128]{3,0,2,1:T(4,128)}, u32[]{:S(2)}) copy-start(f32[3,4,8,128]{3,0,2,1:T(4,128)} %get-tuple-element.576) | copy-start | bytes 147460
  123.3 0.7 copy-start.50
  123.3 0.7 copy-start.86
  (29 other events, 19.0 us)
